TPU v7x, 512 devices: a whole 4x4x16 slice. The times are simulated.
512 devices in a mesh: tm: 32 (over z, core), band: 4 (over y), fsdp: 4 (over x).
Axes of the slice: x: 4, y: 4, z: 16, core: 2. Of those that a mesh axis runs over, the one named last changes fastest.
Arguments:
- video: bfloat16 [128, 64, 128, 256], P('tm', 'band', 'fsdp'), may hold values from -8 to 8
- clip_lengths: int32 [16], replicated, may hold values from 1 to 31, 128 in all
- norm_gains: float32 [2, 256], replicated, may hold values from 0.1 to 1.9
- spatial_kernel_weight: bfloat16 [256, 2304], P(('band', 'fsdp')), may hold values from -0.125 to 0.125
- w_time: bfloat16 [256, 768], P(('band', 'fsdp')), may hold values from -0.21875 to 0.21875
- w_qkv: bfloat16 [256, 768], P(('band', 'fsdp')), may hold values from -4 to 4
- w_out: bfloat16 [256, 256], P(('band', 'fsdp')), may hold values from -0.375 to 0.375
Outputs:
- mixed: bfloat16 [4, 4, 512, 128, 256], P('band', 'fsdp', 'tm')
Inputs may be any that keep to these rules, and one draw needn't show every extreme that they name: `clip_lengths`: every clip has at least one frame and the lengths sum to 128.
All inputs are finite; a program needn't handle non-finite values.
Results may differ from a plain program's by a relative error of at most 0.0064.
Values may be sent and summed in bfloat16 or wider, within the bound.
No kernel may reach another device: no remote copies, remote signals or barrier semaphores. Data moves between devices by JAX's collectives and lax.ppermute only.
A program may use at most 64 MiB of HBM per device.

v0:
```python
import math
import jax
import jax.numpy as jnp
from jax import lax
from jax.sharding import PartitionSpec as P

GROUPS = 32
EPS = 1e-06


def with_halo(x, sides, width):
    for axis, dim in sides:
        size, length = (lax.axis_size(axis), x.shape[dim])
        up = [(i, (i + 1) % size) for i in range(size - 1)]
        down = [(j, i) for i, j in up]
        last = lax.slice_in_dim(x, length - width, length, axis=dim)
        initial = lax.slice_in_dim(x, 0, width, axis=dim)
        before = lax.ppermute(last, axis, up)
        after = lax.ppermute(initial, axis, down)
        x = jnp.concatenate([before, x, after], axis=dim)
    return x


def from_behind(x, axis, by):
    length = lax.axis_size(axis)
    pairs = [(i, i + by) for i in range(length) if 0 <= i + by < length]
    return lax.ppermute(x, axis, pairs)


def butterfly_sum(x, axes):
    for axis in axes:
        size = lax.axis_size(axis)
        step = 1
        while step < size:
            pairs = [(i, i ^ step) for i in range(size)]
            x = x + lax.ppermute(x, axis, pairs)
            step *= 2
    return x


def frame_starts(clip_lengths, total):
    ends = jnp.cumsum(clip_lengths)
    begins = ends - clip_lengths
    index = jnp.arange(total, dtype=jnp.int32)
    chosen = jnp.where(begins[None, :] <= index[:, None], begins[None, :], 0)
    return jnp.max(chosen, axis=1)


def group_moments(field):
    frames, height, width, chans = field.shape
    group_width = chans // GROUPS
    vals = field.astype(jnp.float32).reshape(frames, height * width, GROUPS, group_width)
    sums = jnp.sum(vals, axis=(1, 3))
    squares = jnp.sum(vals * vals, axis=(1, 3))
    both = butterfly_sum(jnp.stack([sums, squares]), ("band", "fsdp"))
    sums, squares = (both[0], both[1])
    count = height * width * group_width * lax.axis_size("band") * lax.axis_size("fsdp")
    mean = sums / count
    scale = lax.rsqrt(squares / count - mean * mean + EPS)
    return (mean, scale)


def apply_norm(field, mean, scale, gain):
    shape = field.shape
    chans = shape[-1]
    group_width = chans // GROUPS
    vals = field.astype(jnp.float32).reshape(shape[0], -1, GROUPS, group_width)
    normed = (vals - mean[:, None, :, None]) * scale[:, None, :, None]
    return normed.reshape(shape) * gain


def body(video, clip_lengths, norm_gains, spatial_kernel_weight, w_time, w_qkv, w_out):
    frames, height, width, chans = video.shape
    widths = [w.shape[1] for w in (spatial_kernel_weight, w_time, w_qkv, w_out)]
    packed = jnp.concatenate([spatial_kernel_weight, w_time, w_qkv, w_out], axis=1)
    gathered = lax.all_gather(packed, ("band", "fsdp"), axis=0, tiled=True)
    offsets = [sum(widths[:i]) for i in range(4)]
    space_full, time_full, qkv_full, output_complete = [
        gathered[:, o : o + w] for o, w in zip(offsets, widths)
    ]
    ranks = lax.axis_size("tm")
    total_frames = frames * ranks
    first = lax.axis_index("tm") * frames
    starts = frame_starts(clip_lengths, total_frames)
    local_starts = lax.dynamic_slice_in_dim(starts, first, frames)
    mean_one, scale_one = group_moments(video)
    act = jax.nn.silu(apply_norm(video, mean_one, scale_one, norm_gains[0])).astype(jnp.bfloat16)
    padded = with_halo(act, (("band", 1), ("fsdp", 2)), 1)
    spatial = jnp.zeros((frames, height, width, chans), jnp.float32)
    for tap in range(9):
        shift_y = tap // 3
        shift_x = tap % 3
        spatial = spatial + jnp.einsum(
            "fhwc,cd->fhwd",
            padded[:, shift_y : shift_y + height, shift_x : shift_x + width],
            space_full[:, tap * chans : (tap + 1) * chans],
            preferred_element_type=jnp.float32,
        )
    spatial = spatial.astype(jnp.bfloat16)
    carried = from_behind(spatial[frames - 2 :], "tm", 1)
    extended = jnp.concatenate([carried, spatial], axis=0)
    position = first + jnp.arange(frames, dtype=jnp.int32)
    slots = jnp.arange(frames + 2, dtype=jnp.int32)
    temporal = jnp.zeros((frames, height, width, chans), jnp.float32)
    for tap in range(3):
        source = jnp.maximum(position - 2 + tap, local_starts) - first + 2
        select = (source[:, None] == slots[None, :]).astype(jnp.bfloat16)
        picked = jnp.einsum(
            "fe,ehwc->fhwc", select, extended, preferred_element_type=jnp.float32
        ).astype(jnp.bfloat16)
        temporal = temporal + jnp.einsum(
            "fhwc,cd->fhwd",
            picked,
            time_full[:, tap * chans : (tap + 1) * chans],
            preferred_element_type=jnp.float32,
        )
    resid = (video.astype(jnp.float32) + temporal).astype(jnp.bfloat16)
    pixels = height * width
    group_pixels = pixels // ranks
    flat_resid = resid.reshape(frames, ranks, group_pixels, chans).transpose(1, 0, 2, 3)
    received = lax.all_to_all(flat_resid, "tm", split_axis=0, concat_axis=0, tiled=True)
    resid_time = received.reshape(total_frames, group_pixels, chans)
    mean_two, scale_two = group_moments(resid)
    mine = jnp.concatenate([mean_two, scale_two], axis=1)
    big = jnp.pad(mine, ((0, 8 - frames), (0, 1024 - 2 * GROUPS)))
    moments = lax.all_gather(big, "tm", axis=0, tiled=True).reshape(ranks, 8, 1024)[
        :, :frames, : 2 * GROUPS
    ]
    moments = moments.reshape(total_frames, 2 * GROUPS)
    mean_all, scale_all = (moments[:, :GROUPS], moments[:, GROUPS:])
    flat_norm = apply_norm(resid_time, mean_all, scale_all, norm_gains[1]).astype(jnp.bfloat16)
    qkv_time = jnp.einsum(
        "fpc,cd->fpd", flat_norm, qkv_full, preferred_element_type=jnp.float32
    ).astype(jnp.bfloat16)
    query = qkv_time[..., :chans]
    keys = qkv_time[..., chans : 2 * chans]
    value_rows = qkv_time[..., 2 * chans :]
    index = jnp.arange(total_frames, dtype=jnp.int32)
    allowed = (index[None, :] <= index[:, None]) & (index[None, :] >= starts[:, None])
    scores = jnp.einsum(
        "fpc,gpc->pfg", query, keys, preferred_element_type=jnp.float32
    ) / math.sqrt(chans)
    scores = jnp.where(allowed[None], scores, -1e30)
    top = jnp.max(scores, axis=-1, keepdims=True)
    expo = jnp.where(allowed[None], jnp.exp(scores - top), 0.0)
    attention_probabilities = (expo / jnp.sum(expo, axis=-1, keepdims=True)).astype(jnp.bfloat16)
    attention_output = jnp.einsum(
        "boh,hba->boa", attention_probabilities, value_rows, preferred_element_type=jnp.float32
    ).astype(jnp.bfloat16)
    projected_output = jnp.einsum(
        "axi,iy->axy", attention_output, output_complete, preferred_element_type=jnp.float32
    )
    mixed = (jnp.swapaxes(resid_time, 0, 1).astype(jnp.float32) + projected_output).astype(
        jnp.bfloat16
    )
    return mixed.reshape(1, 1, mixed.shape[0], total_frames, chans)


def solution(mesh):
    return jax.shard_map(
        body,
        mesh=mesh,
        in_specs=(
            P("tm", "band", "fsdp", None),
            P(),
            P(),
            P(("band", "fsdp"), None),
            P(("band", "fsdp"), None),
            P(("band", "fsdp"), None),
            P(("band", "fsdp"), None),
        ),
        out_specs=P("band", "fsdp", "tm", None, None),
        check_vma=False,
    )
```

profile of v0, /device:TPU:1, one launch (start us, length us, event | category | flops | bytes accessed | tf_op | source)
XLA Modules:
  0.0 233.3 jit_solution(3845554850148898094)
XLA Ops:
  10.2 4.0 %collective-permute-start = (f32[2,4,32]{2,1,0:T(4,128)S(1)}, f32[2,4,32]{2,1,0:T(4,128)S(1)}, u32[]{:S(2)}, u32[]{:S(2)}) collective-permute-start(f32[2,4,32]{2,1,0:T(4,128)S(1)} %pad_maximum_fusion.6), channel_id=1, source_target_pairs={{0,4},{4,0},{8,12},{12,8},{1,5},{5,1},{9,13},{13,9},{2,6},{6,2},{1... | collective-permute-start | bytes 3080 | tf_op jit(solution)/shard_map/ppermute | solution.py:36
  15.2 5.0 %collective-permute-start.1 = (f32[2,4,32]{2,1,0:T(4,128)S(1)}, f32[2,4,32]{2,1,0:T(4,128)S(1)}, u32[]{:S(2)}, u32[]{:S(2)}) collective-permute-start(f32[2,4,32]{2,1,0:T(4,128)S(1)} %fusion.93), channel_id=1, source_target_pairs={{0,8},{4,12},{8,0},{12,4},{1,9},{5,13},{9,1},{13,5},{2,10},{6,14},... | collective-permute-start | bytes 3080 | tf_op jit(solution)/shard_map/ppermute | solution.py:36
  21.2 3.2 %collective-permute-start.2 = (f32[2,4,32]{2,1,0:T(4,128)S(1)}, f32[2,4,32]{2,1,0:T(4,128)S(1)}, u32[]{:S(2)}, u32[]{:S(2)}) collective-permute-start(f32[2,4,32]{2,1,0:T(4,128)S(1)} %fusion.104), channel_id=1, source_target_pairs={{0,1},{1,0},{2,3},{3,2},{4,5},{5,4},{6,7},{7,6},{8,9},{9,8},{10,11... | collective-permute-start | bytes 3080 | tf_op jit(solution)/shard_map/ppermute | solution.py:36
  25.5 4.7 %collective-permute-start.3 = (f32[2,4,32]{2,1,0:T(4,128)S(1)}, f32[2,4,32]{2,1,0:T(4,128)S(1)}, u32[]{:S(2)}, u32[]{:S(2)}) collective-permute-start(f32[2,4,32]{2,1,0:T(4,128)S(1)} %add.111), channel_id=1, source_target_pairs={{0,2},{1,3},{2,0},{3,1},{4,6},{5,7},{6,4},{7,5},{8,10},{9,11},{10,... | collective-permute-start | bytes 3080 | tf_op jit(solution)/shard_map/ppermute | solution.py:36
  32.4 3.2 %collective-permute-start.4 = (bf16[4,1,32,256]{3,2,1,0:T(8,128)(2,1)S(1)}, bf16[4,1,32,256]{3,2,1,0:T(8,128)(2,1)S(1)}, u32[]{:S(2)}, u32[]{:S(2)}) collective-permute-start(bf16[4,1,32,256]{3,2,1,0:T(8,128)(2,1)S(1)} %get-tuple-element.13), channel_id=1, source_target_pairs={{0,4},{4,8},{8,12},{1,5},{5,9},{9,13},{2,6},{6,10},{10,14},{3,7},{... | collective-permute-start | bytes 196616 | tf_op jit(solution)/shard_map/ppermute | solution.py:18
  37.0 4.1 %collective-permute-done.5 = bf16[4,1,32,256]{3,2,1,0:T(8,128)(2,1)S(1)} collective-permute-done((bf16[4,1,32,256]{3,2,1,0:T(8,128)(2,1)S(1)}, bf16[4,1,32,256]{3,2,1,0:T(8,128)(2,1)S(1)}, u32[]{:S(2)}, u32[]{:S(2)}) %collective-permute-start.5) | collective-permute-done | bytes 65568 | tf_op jit(solution)/shard_map/ppermute | solution.py:19
  41.3 3.2 %collective-permute-start.6 = (bf16[4,18,1,256]{3,2,1,0:T(2,128)(2,1)S(1)}, bf16[4,18,1,256]{3,2,1,0:T(2,128)(2,1)S(1)}, u32[]{:S(2)}, u32[]{:S(2)}) collective-permute-start(bf16[4,18,1,256]{3,2,1,0:T(2,128)(2,1)S(1)} %get-tuple-element.12), channel_id=1, source_target_pairs={{0,1},{1,2},{2,3},{4,5},{5,6},{6,7},{8,9},{9,10},{10,11},{12,13},{... | collective-permute-start | bytes 110600 | tf_op jit(solution)/shard_map/ppermute | solution.py:18
  45.9 3.7 %collective-permute-done.7 = bf16[4,18,1,256]{3,2,1,0:T(2,128)(2,1)S(1)} collective-permute-done((bf16[4,18,1,256]{3,2,1,0:T(2,128)(2,1)S(1)}, bf16[4,18,1,256]{3,2,1,0:T(2,128)(2,1)S(1)}, u32[]{:S(2)}, u32[]{:S(2)}) %collective-permute-start.7) | collective-permute-done | bytes 36896 | tf_op jit(solution)/shard_map/ppermute | solution.py:19
  51.3 23.3 %all-gather.3.cloned.1.call-done = bf16[256,4096]{1,0:T(8,128)(2,1)} async-done(((bf16[16,4096]{1,0:T(8,128)(2,1)}), bf16[256,4096]{1,0:T(8,128)(2,1)}) %all-gather.3.cloned.1.call-update) | async-done | bytes 2097168 | tf_op jit(solution)/shard_map/all_gather | solution.py:76
  81.5 5.3 %collective-permute-start.8 = (bf16[2,16,32,256]{3,2,1,0:T(8,128)(2,1)S(1)}, bf16[2,16,32,256]{3,2,1,0:T(8,128)(2,1)S(1)}, u32[]{:S(2)}, u32[]{:S(2)}) collective-permute-start(bf16[2,16,32,256]{3,2,1,0:T(8,128)(2,1)S(1)} %slice.197), channel_id=1, source_target_pairs={{0,16},{16,32},{32,48},{48,64},{64,80},{80,96},{96,112},{112,128},... | collective-permute-start | bytes 1572872 | tf_op jit(solution)/shard_map/ppermute | solution.py:27
  87.2 5.7 %collective-permute-done.8 = bf16[2,16,32,256]{3,2,1,0:T(8,128)(2,1)S(1)} collective-permute-done((bf16[2,16,32,256]{3,2,1,0:T(8,128)(2,1)S(1)}, bf16[2,16,32,256]{3,2,1,0:T(8,128)(2,1)S(1)}, u32[]{:S(2)}, u32[]{:S(2)}) %collective-permute-start.8) | collective-permute-done | bytes 524320 | tf_op jit(solution)/shard_map/ppermute | solution.py:27
  102.3 15.1 %all-to-all-start = ((bf16[32,4,16,256]{3,2,1,0:T(8,128)(2,1)}), bf16[32,4,16,256]{3,2,1,0:T(8,128)(2,1)S(1)}, u32[]{:S(2)}, u32[]{:S(2)}) async-start(bf16[32,4,16,256]{3,2,1,0:T(8,128)(2,1)} %bitcast.135), calls=%async_computation | async-start | bytes 2097152 | tf_op jit(solution)/shard_map/all_to_all | solution.py:121
  117.8 2.8 %collective-permute-start.9 = (f32[2,4,32]{2,1,0:T(4,128)S(1)}, f32[2,4,32]{2,1,0:T(4,128)S(1)}, u32[]{:S(2)}, u32[]{:S(2)}) collective-permute-start(f32[2,4,32]{2,1,0:T(4,128)S(1)} %pad_maximum_fusion.7), channel_id=1, source_target_pairs={{0,4},{4,0},{8,12},{12,8},{1,5},{5,1},{9,13},{13,9},{2,6},{6,2},{1... | collective-permute-start | bytes 3080 | tf_op jit(solution)/shard_map/ppermute | solution.py:36
  120.6 1.8 collective-permute-done.9
  122.5 3.7 %collective-permute-start.10 = (f32[2,4,32]{2,1,0:T(4,128)S(1)}, f32[2,4,32]{2,1,0:T(4,128)S(1)}, u32[]{:S(2)}, u32[]{:S(2)}) collective-permute-start(f32[2,4,32]{2,1,0:T(4,128)S(1)} %fusion.92), channel_id=1, source_target_pairs={{0,8},{4,12},{8,0},{12,4},{1,9},{5,13},{9,1},{13,5},{2,10},{6,14},... | collective-permute-start | bytes 3080 | tf_op jit(solution)/shard_map/ppermute | solution.py:36
  126.2 2.4 %collective-permute-done.10 = f32[2,4,32]{2,1,0:T(4,128)S(1)} collective-permute-done((f32[2,4,32]{2,1,0:T(4,128)S(1)}, f32[2,4,32]{2,1,0:T(4,128)S(1)}, u32[]{:S(2)}, u32[]{:S(2)}) %collective-permute-start.10) | collective-permute-done | bytes 1056 | tf_op jit(solution)/shard_map/ppermute | solution.py:36
  128.6 2.8 %collective-permute-start.11 = (f32[2,4,32]{2,1,0:T(4,128)S(1)}, f32[2,4,32]{2,1,0:T(4,128)S(1)}, u32[]{:S(2)}, u32[]{:S(2)}) collective-permute-start(f32[2,4,32]{2,1,0:T(4,128)S(1)} %fusion.103), channel_id=1, source_target_pairs={{0,1},{1,0},{2,3},{3,2},{4,5},{5,4},{6,7},{7,6},{8,9},{9,8},{10,11... | collective-permute-start | bytes 3080 | tf_op jit(solution)/shard_map/ppermute | solution.py:36
  131.4 1.8 collective-permute-done.11
  133.2 3.7 %collective-permute-start.12 = (f32[2,4,32]{2,1,0:T(4,128)S(1)}, f32[2,4,32]{2,1,0:T(4,128)S(1)}, u32[]{:S(2)}, u32[]{:S(2)}) collective-permute-start(f32[2,4,32]{2,1,0:T(4,128)S(1)} %add.132), channel_id=1, source_target_pairs={{0,2},{1,3},{2,0},{3,1},{4,6},{5,7},{6,4},{7,5},{8,10},{9,11},{10,... | collective-permute-start | bytes 3080 | tf_op jit(solution)/shard_map/ppermute | solution.py:36
  137.0 2.4 %collective-permute-done.12 = f32[2,4,32]{2,1,0:T(4,128)S(1)} collective-permute-done((f32[2,4,32]{2,1,0:T(4,128)S(1)}, f32[2,4,32]{2,1,0:T(4,128)S(1)}, u32[]{:S(2)}, u32[]{:S(2)}) %collective-permute-start.12) | collective-permute-done | bytes 1056 | tf_op jit(solution)/shard_map/ppermute | solution.py:36
  140.1 73.9 %all-gather.5.cloned.1.call-done = f32[256,1024]{1,0:T(8,128)} async-done(((f32[8,1024]{1,0:T(8,128)}), f32[256,1024]{1,0:T(8,128)}) %all-gather.5.cloned.1.call-update) | async-done | bytes 1048592 | tf_op jit(solution)/shard_map/all_gather | solution.py:126
  215.8 4.6 %convolution_convert_fusion = bf16[128,16,768]{2,0,1:T(8,128)(2,1)} fusion(f32[128,16,256]{2,1,0:T(8,128)S(1)} %bitcast_convert_fusion, f32[256]{0:T(256)S(1)} %bitcast.150, f32[128,256]{1,0:T(8,128)S(1)} %copy.42, f32[128,256]{1,0:T(8,128)S(1)} %copy.40, bf16[256,4096]{1,0:T(8,128)(2,1)} %all-gather.3.cloned.1.call-done), kind=kOutput, calls=%fused_computation.7 | convolution fusion | flops 808976384 | bytes 5899264 | tf_op jit(solution)/shard_map/fpc,cd->fpd/dot_general | solution.py:132
  220.4 2.1 fusion.97
  222.5 3.9 %fusion.31 = bf16[1,1,16,128,256]{4,3,2,1,0:T(8,128)(2,1)} fusion(f32[128,16,256]{2,1,0:T(8,128)S(1)} %bitcast_convert_fusion, bf16[128,16,768]{2,0,1:T(8,128)(2,1)} %convolution_convert_fusion, f32[16,128,128]{1,2,0:T(8,128)S(1)} %get-tuple-element.24, f32[16,128]{1,0:T(8,128)S(1)} %get-tuple-element.23, bf16[256,4096]{1,0:T(8,128)(2,1)} %all-gather.3.cloned.1.call-done), kind=kOutput, calls=%fused_computation.39 | convolution fusion | flops 404750336 | bytes 5382144 | tf_op jit(solution)/shard_map/axi,iy->axy/dot_general | solution.py:150
  (91 shorter events, 33.0 us)
Async XLA Ops:
  6.5 25.2 %copy-start.1 = (bf16[4,16,32,256]{3,2,1,0:T(8,128)(2,1)S(1)}, bf16[4,16,32,256]{3,2,1,0:T(8,128)(2,1)}, u32[]{:S(2)}) copy-start(bf16[4,16,32,256]{3,2,1,0:T(8,128)(2,1)} %param.7) | copy-start | bytes 3145732
  6.5 68.1 %all-gather.3.cloned.1.call-start = ((), (), s32[]{:S(2)}) async-start(), calls=%async_computation.1 | async-start | bytes 2228224 | tf_op jit(solution)/shard_map/all_gather | solution.py:76
  10.2 5.0 %collective-permute-start = (f32[2,4,32]{2,1,0:T(4,128)S(1)}, f32[2,4,32]{2,1,0:T(4,128)S(1)}, u32[]{:S(2)}, u32[]{:S(2)}) collective-permute-start(f32[2,4,32]{2,1,0:T(4,128)S(1)} %pad_maximum_fusion.6), channel_id=1, source_target_pairs={{0,4},{4,0},{8,12},{12,8},{1,5},{5,1},{9,13},{13,9},{2,6},{6,2},{1... | collective-permute-start | bytes 3080 | tf_op jit(solution)/shard_map/ppermute | solution.py:36
  15.2 6.0 %collective-permute-start.1 = (f32[2,4,32]{2,1,0:T(4,128)S(1)}, f32[2,4,32]{2,1,0:T(4,128)S(1)}, u32[]{:S(2)}, u32[]{:S(2)}) collective-permute-start(f32[2,4,32]{2,1,0:T(4,128)S(1)} %fusion.93), channel_id=1, source_target_pairs={{0,8},{4,12},{8,0},{12,4},{1,9},{5,13},{9,1},{13,5},{2,10},{6,14},... | collective-permute-start | bytes 3080 | tf_op jit(solution)/shard_map/ppermute | solution.py:36
  21.2 4.3 %collective-permute-start.2 = (f32[2,4,32]{2,1,0:T(4,128)S(1)}, f32[2,4,32]{2,1,0:T(4,128)S(1)}, u32[]{:S(2)}, u32[]{:S(2)}) collective-permute-start(f32[2,4,32]{2,1,0:T(4,128)S(1)} %fusion.104), channel_id=1, source_target_pairs={{0,1},{1,0},{2,3},{3,2},{4,5},{5,4},{6,7},{7,6},{8,9},{9,8},{10,11... | collective-permute-start | bytes 3080 | tf_op jit(solution)/shard_map/ppermute | solution.py:36
  25.5 5.8 %collective-permute-start.3 = (f32[2,4,32]{2,1,0:T(4,128)S(1)}, f32[2,4,32]{2,1,0:T(4,128)S(1)}, u32[]{:S(2)}, u32[]{:S(2)}) collective-permute-start(f32[2,4,32]{2,1,0:T(4,128)S(1)} %add.111), channel_id=1, source_target_pairs={{0,2},{1,3},{2,0},{3,1},{4,6},{5,7},{6,4},{7,5},{8,10},{9,11},{10,... | collective-permute-start | bytes 3080 | tf_op jit(solution)/shard_map/ppermute | solution.py:36
  32.4 4.6 %collective-permute-start.4 = (bf16[4,1,32,256]{3,2,1,0:T(8,128)(2,1)S(1)}, bf16[4,1,32,256]{3,2,1,0:T(8,128)(2,1)S(1)}, u32[]{:S(2)}, u32[]{:S(2)}) collective-permute-start(bf16[4,1,32,256]{3,2,1,0:T(8,128)(2,1)S(1)} %get-tuple-element.13), channel_id=1, source_target_pairs={{0,4},{4,8},{8,12},{1,5},{5,9},{9,13},{2,6},{6,10},{10,14},{3,7},{... | collective-permute-start | bytes 196616 | tf_op jit(solution)/shard_map/ppermute | solution.py:18
  35.7 5.4 %collective-permute-start.5 = (bf16[4,1,32,256]{3,2,1,0:T(8,128)(2,1)S(1)}, bf16[4,1,32,256]{3,2,1,0:T(8,128)(2,1)S(1)}, u32[]{:S(2)}, u32[]{:S(2)}) collective-permute-start(bf16[4,1,32,256]{3,2,1,0:T(8,128)(2,1)S(1)} %get-tuple-element.14), channel_id=1, source_target_pairs={{4,0},{8,4},{12,8},{5,1},{9,5},{13,9},{6,2},{10,6},{14,10},{7,3},{... | collective-permute-start | bytes 196616 | tf_op jit(solution)/shard_map/ppermute | solution.py:19
  41.3 4.6 %collective-permute-start.6 = (bf16[4,18,1,256]{3,2,1,0:T(2,128)(2,1)S(1)}, bf16[4,18,1,256]{3,2,1,0:T(2,128)(2,1)S(1)}, u32[]{:S(2)}, u32[]{:S(2)}) collective-permute-start(bf16[4,18,1,256]{3,2,1,0:T(2,128)(2,1)S(1)} %get-tuple-element.12), channel_id=1, source_target_pairs={{0,1},{1,2},{2,3},{4,5},{5,6},{6,7},{8,9},{9,10},{10,11},{12,13},{... | collective-permute-start | bytes 110600 | tf_op jit(solution)/shard_map/ppermute | solution.py:18
  44.5 5.1 %collective-permute-start.7 = (bf16[4,18,1,256]{3,2,1,0:T(2,128)(2,1)S(1)}, bf16[4,18,1,256]{3,2,1,0:T(2,128)(2,1)S(1)}, u32[]{:S(2)}, u32[]{:S(2)}) collective-permute-start(bf16[4,18,1,256]{3,2,1,0:T(2,128)(2,1)S(1)} %get-tuple-element.11), channel_id=1, source_target_pairs={{1,0},{2,1},{3,2},{5,4},{6,5},{7,6},{9,8},{10,9},{11,10},{13,12},{... | collective-permute-start | bytes 110600 | tf_op jit(solution)/shard_map/ppermute | solution.py:19
  74.6 1.7 copy-start.3
  76.3 1.4 copy-start
  80.4 6.4 %copy-start.4 = (s32[16]{0:T(128)S(1)}, s32[16]{0:T(128)}, u32[]{:S(2)}) copy-start(s32[16]{0:T(128)} %param.8) | copy-start | bytes 196
  81.5 11.4 %collective-permute-start.8 = (bf16[2,16,32,256]{3,2,1,0:T(8,128)(2,1)S(1)}, bf16[2,16,32,256]{3,2,1,0:T(8,128)(2,1)S(1)}, u32[]{:S(2)}, u32[]{:S(2)}) collective-permute-start(bf16[2,16,32,256]{3,2,1,0:T(8,128)(2,1)S(1)} %slice.197), channel_id=1, source_target_pairs={{0,16},{16,32},{32,48},{48,64},{64,80},{80,96},{96,112},{112,128},... | collective-permute-start | bytes 1572872 | tf_op jit(solution)/shard_map/ppermute | solution.py:27
  98.0 1.4 copy-start.2
  102.3 113.1 %all-to-all-start = ((bf16[32,4,16,256]{3,2,1,0:T(8,128)(2,1)}), bf16[32,4,16,256]{3,2,1,0:T(8,128)(2,1)S(1)}, u32[]{:S(2)}, u32[]{:S(2)}) async-start(bf16[32,4,16,256]{3,2,1,0:T(8,128)(2,1)} %bitcast.135), calls=%async_computation | async-start | bytes 2097152 | tf_op jit(solution)/shard_map/all_to_all | solution.py:121
  117.4 96.7 %all-gather.5.cloned.1.call-start = ((), (), s32[]{:S(2)}) async-start(), calls=%async_computation.2 | async-start | bytes 1081344 | tf_op jit(solution)/shard_map/all_gather | solution.py:126
  117.8 4.6 %collective-permute-start.9 = (f32[2,4,32]{2,1,0:T(4,128)S(1)}, f32[2,4,32]{2,1,0:T(4,128)S(1)}, u32[]{:S(2)}, u32[]{:S(2)}) collective-permute-start(f32[2,4,32]{2,1,0:T(4,128)S(1)} %pad_maximum_fusion.7), channel_id=1, source_target_pairs={{0,4},{4,0},{8,12},{12,8},{1,5},{5,1},{9,13},{13,9},{2,6},{6,2},{1... | collective-permute-start | bytes 3080 | tf_op jit(solution)/shard_map/ppermute | solution.py:36
  122.5 6.1 %collective-permute-start.10 = (f32[2,4,32]{2,1,0:T(4,128)S(1)}, f32[2,4,32]{2,1,0:T(4,128)S(1)}, u32[]{:S(2)}, u32[]{:S(2)}) collective-permute-start(f32[2,4,32]{2,1,0:T(4,128)S(1)} %fusion.92), channel_id=1, source_target_pairs={{0,8},{4,12},{8,0},{12,4},{1,9},{5,13},{9,1},{13,5},{2,10},{6,14},... | collective-permute-start | bytes 3080 | tf_op jit(solution)/shard_map/ppermute | solution.py:36
  128.6 4.6 %collective-permute-start.11 = (f32[2,4,32]{2,1,0:T(4,128)S(1)}, f32[2,4,32]{2,1,0:T(4,128)S(1)}, u32[]{:S(2)}, u32[]{:S(2)}) collective-permute-start(f32[2,4,32]{2,1,0:T(4,128)S(1)} %fusion.103), channel_id=1, source_target_pairs={{0,1},{1,0},{2,3},{3,2},{4,5},{5,4},{6,7},{7,6},{8,9},{9,8},{10,11... | collective-permute-start | bytes 3080 | tf_op jit(solution)/shard_map/ppermute | solution.py:36
  133.2 6.1 %collective-permute-start.12 = (f32[2,4,32]{2,1,0:T(4,128)S(1)}, f32[2,4,32]{2,1,0:T(4,128)S(1)}, u32[]{:S(2)}, u32[]{:S(2)}) collective-permute-start(f32[2,4,32]{2,1,0:T(4,128)S(1)} %add.132), channel_id=1, source_target_pairs={{0,2},{1,3},{2,0},{3,1},{4,6},{5,7},{6,4},{7,5},{8,10},{9,11},{10,... | collective-permute-start | bytes 3080 | tf_op jit(solution)/shard_map/ppermute | solution.py:36
Sparse Core Ops, SparseCore 0:
  10.3 64.2 all-gather.2
  140.2 73.7 all-gather.4
where the time goes:
time: 234 us; the launch traced here: 233 us
  waiting for transfers between devices  123 us (53%)
  starting transfers between devices  59.3 us (25%)
  matrix products  24.5 us (10%)
  between operations  13.8 us (6%)
  other arithmetic  7.72 us (3%)
  local copies, waits for them, and re-layouts  5.18 us (2%)
    all_gather x1, waiting for transfers between devices, body(): lax.all_gather(big, 'tm', axis=0, tiled=True).reshape(ranks, 8, 1024)  73.9 us
    ppermute x8, starting transfers between devices, butterfly_sum(): x = x + lax.ppermute(x, axis, pairs)  29.9 us
    all_gather x1, waiting for transfers between devices, body(): gathered = lax.all_gather(packed, ('band', 'fsdp'), axis=0, tiled=True)  23.3 us
    all_to_all x1, starting transfers between devices, body(): lax.all_to_all(flat_resid, 'tm', split_axis=0, concat_axis=0, tiled=True)  15.1 us
    ppermute x8, waiting for transfers between devices, butterfly_sum(): x = x + lax.ppermute(x, axis, pairs)  12 us
    ppermute x2, waiting for transfers between devices, with_halo(): after = lax.ppermute(initial, axis, down)  7.84 us
    ppermute x2, starting transfers between devices, with_halo(): before = lax.ppermute(last, axis, up)  6.45 us
    dot_general x9, matrix products, body(): jnp.einsum('fhwc,cd->fhwd', padded[:, shift_y:shift_y + height, shift_x:s...  5.7 us
  transfers between devices with their start and end apart: 16, of which 14 were waited for; matrix products, arithmetic and copies ran while one was open for 4% of the time, Pallas kernels for 0%

commit v1 on v0

--- a/solution.py
+++ b/solution.py
@@ -6,6 +6,28 @@
 
 GROUPS = 32
 EPS = 1e-06
+
+
+def joined_along(blocks, dim):
+    dims = list(blocks.shape[1:])
+    dims[dim] *= blocks.shape[0]
+    return jnp.moveaxis(blocks, 0, dim).reshape(dims)
+
+
+def collect(x, axis, dim):
+    size = lax.axis_size(axis)
+    pairs = [(i, (i + 1) % size) for i in range(size)]
+    back = [(b, a) for a, b in pairs]
+    lower, upper = ([], [])
+    for step in range(size - 1):
+        if step % 2 == 0:
+            lower.append(lax.ppermute(lower[-1] if lower else x, axis, pairs))
+        else:
+            upper.append(lax.ppermute(upper[-1] if upper else x, axis, back))
+    blocks = jnp.stack([*lower[::-1], x, *upper])
+    shift = lax.axis_index(axis) - len(lower)
+    blocks = blocks[(jnp.arange(size) - shift) % size]
+    return joined_along(blocks, dim)
 
 
 def with_halo(x, sides, width):
@@ -73,7 +95,7 @@
     frames, height, width, chans = video.shape
     widths = [w.shape[1] for w in (spatial_kernel_weight, w_time, w_qkv, w_out)]
     packed = jnp.concatenate([spatial_kernel_weight, w_time, w_qkv, w_out], axis=1)
-    gathered = lax.all_gather(packed, ("band", "fsdp"), axis=0, tiled=True)
+    gathered = collect(packed, ("band", "fsdp"), 0)
     offsets = [sum(widths[:i]) for i in range(4)]
     space_full, time_full, qkv_full, output_complete = [
         gathered[:, o : o + w] for o, w in zip(offsets, widths)

time: 234 us -> 293 us (1.25)
  starting transfers between devices: 59.3 us -> 120 us
  waiting for transfers between devices: 123 us -> 98.3 us
  local copies, waits for them, and re-layouts: 5.18 us -> 21.3 us
  matrix products: 24.5 us -> 31.8 us
    ppermute x0 -> x15, starting transfers between devices: none -> 60.9 us  [the longest x7 44.4 us: collect(): upper.append(lax.ppermute(upper[-1] if upper else x, axis, back))]
    all_gather x1 -> x0, waiting for transfers between devices: 23.3 us -> none  [body(): gathered = lax.all_gather(packed, ('band', 'fsdp'), axis=0, tiled=True)]
    unnamed x12 -> x32, local copies, waits for them, and re-layouts: 1.2 us -> 12.4 us
    ppermute x8, starting transfers between devices: 29.9 us -> 21.2 us  [butterfly_sum(): x = x + lax.ppermute(x, axis, pairs)]
    ppermute x2, waiting for transfers between devices: 7.84 us -> 0.01 us  [with_halo(): after = lax.ppermute(initial, axis, down)]
    dot_general x9, matrix products: 5.7 us -> 13.2 us  [body(): jnp.einsum('fhwc,cd->fhwd', padded[:, shift_y:shift_y + height, shift_x:s...]
    ppermute x1, starting transfers between devices: 5.27 us -> 12.2 us  [from_behind(): return lax.ppermute(x, axis, pairs)]
    ppermute x0 -> x15, waiting for transfers between devices: none -> 5.85 us  [the longest x8 5.83 us: collect(): lower.append(lax.ppermute(lower[-1] if lower else x, axis, pairs))]
  transfers between devices with their start and end apart: 16 -> 30, of which waited for: 14 -> 11; matrix products, arithmetic and copies ran while one was open for 4% -> 7% of each run, Pallas kernels for 0% -> 0%
where the time goes in v1:
time: 293 us; the launch traced here: 291 us
  starting transfers between devices  120 us (41%)
  waiting for transfers between devices  98.3 us (34%)
  matrix products  31.8 us (11%)
  local copies, waits for them, and re-layouts  21.3 us (7%)
  between operations  14.1 us (5%)
  other arithmetic  6.17 us (2%)
    all_gather x1, waiting for transfers between devices, body(): lax.all_gather(big, 'tm', axis=0, tiled=True).reshape(ranks, 8, 1024)  71.9 us
    ppermute x7, starting transfers between devices, collect(): upper.append(lax.ppermute(upper[-1] if upper else x, axis, back))  44.4 us
    ppermute x8, starting transfers between devices, butterfly_sum(): x = x + lax.ppermute(x, axis, pairs)  21.2 us
    all_to_all x1, starting transfers between devices, body(): lax.all_to_all(flat_resid, 'tm', split_axis=0, concat_axis=0, tiled=True)  17.4 us
    ppermute x8, starting transfers between devices, collect(): lower.append(lax.ppermute(lower[-1] if lower else x, axis, pairs))  16.5 us
    ppermute x8, waiting for transfers between devices, butterfly_sum(): x = x + lax.ppermute(x, axis, pairs)  15.1 us
    dot_general x9, matrix products, body(): jnp.einsum('fhwc,cd->fhwd', padded[:, shift_y:shift_y + height, shift_x:s...  13.2 us
    unnamed x32, local copies, waits for them, and re-layouts  12.4 us
  transfers between devices with their start and end apart: 30, of which 11 were waited for; matrix products, arithmetic and copies ran while one was open for 7% of the time, Pallas kernels for 0%

profile of v1, /device:TPU:1, one launch (start us, length us, event | category | flops | bytes accessed | tf_op | source)
XLA Modules:
  0.0 291.3 jit_solution(13787952974042604179)
XLA Ops:
  8.5 4.0 %collective-permute-start = (f32[2,4,32]{2,1,0:T(4,128)S(1)}, f32[2,4,32]{2,1,0:T(4,128)S(1)}, u32[]{:S(2)}, u32[]{:S(2)}) collective-permute-start(f32[2,4,32]{2,1,0:T(4,128)S(1)} %pad_maximum_fusion.5), channel_id=1, source_target_pairs={{0,4},{4,0},{8,12},{12,8},{1,5},{5,1},{9,13},{13,9},{2,6},{6,2},{1... | collective-permute-start | bytes 3080 | tf_op jit(solution)/shard_map/ppermute | solution.py:58
  15.0 4.5 %collective-permute-start.1 = (f32[2,4,32]{2,1,0:T(4,128)S(1)}, f32[2,4,32]{2,1,0:T(4,128)S(1)}, u32[]{:S(2)}, u32[]{:S(2)}) collective-permute-start(f32[2,4,32]{2,1,0:T(4,128)S(1)} %fusion.95), channel_id=1, source_target_pairs={{0,8},{4,12},{8,0},{12,4},{1,9},{5,13},{9,1},{13,5},{2,10},{6,14},... | collective-permute-start | bytes 3080 | tf_op jit(solution)/shard_map/ppermute | solution.py:58
  20.2 3.1 %collective-permute-start.7 = (bf16[16,4096]{1,0:T(8,128)(2,1)S(1)}, bf16[16,4096]{1,0:T(8,128)(2,1)S(1)}, u32[]{:S(2)}, u32[]{:S(2)}) collective-permute-start(bf16[16,4096]{1,0:T(8,128)(2,1)S(1)} %constant_dynamic-update-slice_fusion), channel_id=1, source_target_pairs={{0,1},{1,2},{2,3},{3,4},{4,5},{5,6},{6,7},{7,8},{8,9},{9,10},{10,1... | collective-permute-start | bytes 393224 | tf_op jit(solution)/shard_map/ppermute | solution.py:24
  23.3 3.1 %collective-permute-start.2 = (f32[2,4,32]{2,1,0:T(4,128)S(1)}, f32[2,4,32]{2,1,0:T(4,128)S(1)}, u32[]{:S(2)}, u32[]{:S(2)}) collective-permute-start(f32[2,4,32]{2,1,0:T(4,128)S(1)} %fusion.106), channel_id=1, source_target_pairs={{0,1},{1,0},{2,3},{3,2},{4,5},{5,4},{6,7},{7,6},{8,9},{9,8},{10,11... | collective-permute-start | bytes 3080 | tf_op jit(solution)/shard_map/ppermute | solution.py:58
  26.5 4.3 %collective-permute-start.15 = (bf16[16,4096]{1,0:T(8,128)(2,1)S(1)}, bf16[16,4096]{1,0:T(8,128)(2,1)S(1)}, u32[]{:S(2)}, u32[]{:S(2)}) collective-permute-start(bf16[16,4096]{1,0:T(8,128)(2,1)S(1)} %constant_dynamic-update-slice_fusion), channel_id=1, source_target_pairs={{1,0},{2,1},{3,2},{4,3},{5,4},{6,5},{7,6},{8,7},{9,8},{10,9},{11,1... | collective-permute-start | bytes 393224 | tf_op jit(solution)/shard_map/ppermute | solution.py:26
  36.6 5.1 %collective-permute-done.8 = bf16[16,4096]{1,0:T(8,128)(2,1)S(1)} collective-permute-done((bf16[16,4096]{1,0:T(8,128)(2,1)S(1)}, bf16[16,4096]{1,0:T(8,128)(2,1)S(1)}, u32[]{:S(2)}, u32[]{:S(2)}) %collective-permute-start.8) | collective-permute-done | bytes 131104 | tf_op jit(solution)/shard_map/ppermute | solution.py:24
  43.9 6.7 %collective-permute-start.16 = (bf16[16,4096]{1,0:T(8,128)(2,1)S(1)}, bf16[16,4096]{1,0:T(8,128)(2,1)S(1)}, u32[]{:S(2)}, u32[]{:S(2)}) collective-permute-start(bf16[16,4096]{1,0:T(8,128)(2,1)S(1)} %collective-permute-done.15), channel_id=1, source_target_pairs={{1,0},{2,1},{3,2},{4,3},{5,4},{6,5},{7,6},{8,7},{9,8},{10,9},{11,1... | collective-permute-start | bytes 393224 | tf_op jit(solution)/shard_map/ppermute | solution.py:26
  52.9 6.7 %collective-permute-start.17 = (bf16[16,4096]{1,0:T(8,128)(2,1)S(1)}, bf16[16,4096]{1,0:T(8,128)(2,1)S(1)}, u32[]{:S(2)}, u32[]{:S(2)}) collective-permute-start(bf16[16,4096]{1,0:T(8,128)(2,1)S(1)} %collective-permute-done.16), channel_id=1, source_target_pairs={{1,0},{2,1},{3,2},{4,3},{5,4},{6,5},{7,6},{8,7},{9,8},{10,9},{11,1... | collective-permute-start | bytes 393224 | tf_op jit(solution)/shard_map/ppermute | solution.py:26
  62.4 6.7 %collective-permute-start.18 = (bf16[16,4096]{1,0:T(8,128)(2,1)S(1)}, bf16[16,4096]{1,0:T(8,128)(2,1)S(1)}, u32[]{:S(2)}, u32[]{:S(2)}) collective-permute-start(bf16[16,4096]{1,0:T(8,128)(2,1)S(1)} %collective-permute-done.17), channel_id=1, source_target_pairs={{1,0},{2,1},{3,2},{4,3},{5,4},{6,5},{7,6},{8,7},{9,8},{10,9},{11,1... | collective-permute-start | bytes 393224 | tf_op jit(solution)/shard_map/ppermute | solution.py:26
  73.9 9.4 %collective-permute-start.19 = (bf16[16,4096]{1,0:T(8,128)(2,1)S(1)}, bf16[16,4096]{1,0:T(8,128)(2,1)S(1)}, u32[]{:S(2)}, u32[]{:S(2)}) collective-permute-start(bf16[16,4096]{1,0:T(8,128)(2,1)S(1)} %collective-permute-done.18), channel_id=1, source_target_pairs={{1,0},{2,1},{3,2},{4,3},{5,4},{6,5},{7,6},{8,7},{9,8},{10,9},{11,1... | collective-permute-start | bytes 393224 | tf_op jit(solution)/shard_map/ppermute | solution.py:26
  86.7 4.0 %collective-permute-start.6 = (bf16[4,18,1,256]{3,2,1,0:T(2,128)(2,1)S(1)}, bf16[4,18,1,256]{3,2,1,0:T(2,128)(2,1)S(1)}, u32[]{:S(2)}, u32[]{:S(2)}) collective-permute-start(bf16[4,18,1,256]{3,2,1,0:T(2,128)(2,1)S(1)} %get-tuple-element.12), channel_id=1, source_target_pairs={{0,1},{1,2},{2,3},{4,5},{5,6},{6,7},{8,9},{9,10},{10,11},{12,13},{... | collective-permute-start | bytes 110600 | tf_op jit(solution)/shard_map/ppermute | solution.py:40
  90.7 4.0 %collective-permute-start.20 = (bf16[16,4096]{1,0:T(8,128)(2,1)S(1)}, bf16[16,4096]{1,0:T(8,128)(2,1)S(1)}, u32[]{:S(2)}, u32[]{:S(2)}) collective-permute-start(bf16[16,4096]{1,0:T(8,128)(2,1)S(1)} %collective-permute-done.19), channel_id=1, source_target_pairs={{1,0},{2,1},{3,2},{4,3},{5,4},{6,5},{7,6},{8,7},{9,8},{10,9},{11,1... | collective-permute-start | bytes 393224 | tf_op jit(solution)/shard_map/ppermute | solution.py:26
  98.5 6.7 %collective-permute-start.21 = (bf16[16,4096]{1,0:T(8,128)(2,1)S(1)}, bf16[16,4096]{1,0:T(8,128)(2,1)S(1)}, u32[]{:S(2)}, u32[]{:S(2)}) collective-permute-start(bf16[16,4096]{1,0:T(8,128)(2,1)S(1)} %collective-permute-done.20), channel_id=1, source_target_pairs={{1,0},{2,1},{3,2},{4,3},{5,4},{6,5},{7,6},{8,7},{9,8},{10,9},{11,1... | collective-permute-start | bytes 393224 | tf_op jit(solution)/shard_map/ppermute | solution.py:26
  115.7 3.6 %gather_fusion = bf16[16,16,4096]{2,1,0:T(8,128)(2,1)} fusion(bf16[16,16,4096]{2,1,0:T(8,128)(2,1)} %bitcast_dynamic-update-slice_fusion, s32[1024]{0:T(1024)S(1)} %pad_clamp_fusion), kind=kCustom, calls=%fused_computation | custom fusion | bytes 4194368 | tf_op jit(solution)/shard_map/gather | solution.py:29
  132.6 12.2 %collective-permute-start.23 = (bf16[2,16,32,256]{3,2,1,0:T(8,128)(2,1)S(1)}, bf16[2,16,32,256]{3,2,1,0:T(8,128)(2,1)S(1)}, u32[]{:S(2)}, u32[]{:S(2)}) collective-permute-start(bf16[2,16,32,256]{3,2,1,0:T(8,128)(2,1)S(1)} %slice.199), channel_id=1, source_target_pairs={{0,16},{16,32},{32,48},{48,64},{64,80},{80,96},{96,112},{112,128},... | collective-permute-start | bytes 1572872 | tf_op jit(solution)/shard_map/ppermute | solution.py:49
  145.3 5.5 %collective-permute-done.23 = bf16[2,16,32,256]{3,2,1,0:T(8,128)(2,1)S(1)} collective-permute-done((bf16[2,16,32,256]{3,2,1,0:T(8,128)(2,1)S(1)}, bf16[2,16,32,256]{3,2,1,0:T(8,128)(2,1)S(1)}, u32[]{:S(2)}, u32[]{:S(2)}) %collective-permute-start.23) | collective-permute-done | bytes 524320 | tf_op jit(solution)/shard_map/ppermute | solution.py:49
  160.1 17.4 %all-to-all-start = ((bf16[32,4,16,256]{3,2,1,0:T(8,128)(2,1)}), bf16[32,4,16,256]{3,2,1,0:T(8,128)(2,1)S(1)}, u32[]{:S(2)}, u32[]{:S(2)}) async-start(bf16[32,4,16,256]{3,2,1,0:T(8,128)(2,1)} %bitcast.170), calls=%async_computation | async-start | bytes 2097152 | tf_op jit(solution)/shard_map/all_to_all | solution.py:143
  179.9 2.7 collective-permute-done.24
  184.5 4.2 %collective-permute-done.25 = f32[2,4,32]{2,1,0:T(4,128)S(1)} collective-permute-done((f32[2,4,32]{2,1,0:T(4,128)S(1)}, f32[2,4,32]{2,1,0:T(4,128)S(1)}, u32[]{:S(2)}, u32[]{:S(2)}) %collective-permute-start.25) | collective-permute-done | bytes 1056 | tf_op jit(solution)/shard_map/ppermute | solution.py:58
  190.6 2.7 collective-permute-done.26
  195.3 4.2 %collective-permute-done.27 = f32[2,4,32]{2,1,0:T(4,128)S(1)} collective-permute-done((f32[2,4,32]{2,1,0:T(4,128)S(1)}, f32[2,4,32]{2,1,0:T(4,128)S(1)}, u32[]{:S(2)}, u32[]{:S(2)}) %collective-permute-start.27) | collective-permute-done | bytes 1056 | tf_op jit(solution)/shard_map/ppermute | solution.py:58
  200.3 71.9 %all-gather.2.cloned.1.call-done = f32[256,1024]{1,0:T(8,128)} async-done(((f32[8,1024]{1,0:T(8,128)}), f32[256,1024]{1,0:T(8,128)}) %all-gather.2.cloned.1.call-update) | async-done | bytes 1048592 | tf_op jit(solution)/shard_map/all_gather | solution.py:148
  273.9 4.6 %convolution_convert_fusion = bf16[128,16,768]{2,0,1:T(8,128)(2,1)} fusion(f32[128,16,256]{2,1,0:T(8,128)S(1)} %bitcast_convert_fusion, f32[256]{0:T(256)S(1)} %bitcast.199, f32[128,256]{1,0:T(8,128)S(1)} %copy.42, f32[128,256]{1,0:T(8,128)S(1)} %copy.40, bf16[256,4096]{1,0:T(8,128)(2,1)} %bitcast.183), kind=kOutput, calls=%fused_computation.8 | convolution fusion | flops 808976384 | bytes 5899264 | tf_op jit(solution)/shard_map/fpc,cd->fpd/dot_general | solution.py:154
  280.6 3.9 %fusion.31 = bf16[1,1,16,128,256]{4,3,2,1,0:T(8,128)(2,1)} fusion(f32[128,16,256]{2,1,0:T(8,128)S(1)} %bitcast_convert_fusion, bf16[128,16,768]{2,0,1:T(8,128)(2,1)} %convolution_convert_fusion, f32[16,128,128]{1,2,0:T(8,128)S(1)} %get-tuple-element.24, f32[16,128]{1,0:T(8,128)S(1)} %get-tuple-element.23, bf16[256,4096]{1,0:T(8,128)(2,1)} %bitcast.184), kind=kOutput, calls=%fused_computation.40 | convolution fusion | flops 404750336 | bytes 5382144 | tf_op jit(solution)/shard_map/axi,iy->axy/dot_general | solution.py:172
  (142 shorter events, 76.1 us)
Async XLA Ops:
  15.0 8.4 %collective-permute-start.1 = (f32[2,4,32]{2,1,0:T(4,128)S(1)}, f32[2,4,32]{2,1,0:T(4,128)S(1)}, u32[]{:S(2)}, u32[]{:S(2)}) collective-permute-start(f32[2,4,32]{2,1,0:T(4,128)S(1)} %fusion.95), channel_id=1, source_target_pairs={{0,8},{4,12},{8,0},{12,4},{1,9},{5,13},{9,1},{13,5},{2,10},{6,14},... | collective-permute-start | bytes 3080 | tf_op jit(solution)/shard_map/ppermute | solution.py:58
  20.2 12.5 %collective-permute-start.7 = (bf16[16,4096]{1,0:T(8,128)(2,1)S(1)}, bf16[16,4096]{1,0:T(8,128)(2,1)S(1)}, u32[]{:S(2)}, u32[]{:S(2)}) collective-permute-start(bf16[16,4096]{1,0:T(8,128)(2,1)S(1)} %constant_dynamic-update-slice_fusion), channel_id=1, source_target_pairs={{0,1},{1,2},{2,3},{3,4},{4,5},{5,6},{6,7},{7,8},{8,9},{9,10},{10,1... | collective-permute-start | bytes 393224 | tf_op jit(solution)/shard_map/ppermute | solution.py:24
  23.3 7.4 %collective-permute-start.2 = (f32[2,4,32]{2,1,0:T(4,128)S(1)}, f32[2,4,32]{2,1,0:T(4,128)S(1)}, u32[]{:S(2)}, u32[]{:S(2)}) collective-permute-start(f32[2,4,32]{2,1,0:T(4,128)S(1)} %fusion.106), channel_id=1, source_target_pairs={{0,1},{1,0},{2,3},{3,2},{4,5},{5,4},{6,7},{7,6},{8,9},{9,8},{10,11... | collective-permute-start | bytes 3080 | tf_op jit(solution)/shard_map/ppermute | solution.py:58
  26.5 17.4 %collective-permute-start.15 = (bf16[16,4096]{1,0:T(8,128)(2,1)S(1)}, bf16[16,4096]{1,0:T(8,128)(2,1)S(1)}, u32[]{:S(2)}, u32[]{:S(2)}) collective-permute-start(bf16[16,4096]{1,0:T(8,128)(2,1)S(1)} %constant_dynamic-update-slice_fusion), channel_id=1, source_target_pairs={{1,0},{2,1},{3,2},{4,3},{5,4},{6,5},{7,6},{8,7},{9,8},{10,9},{11,1... | collective-permute-start | bytes 393224 | tf_op jit(solution)/shard_map/ppermute | solution.py:26
  32.7 9.0 %collective-permute-start.8 = (bf16[16,4096]{1,0:T(8,128)(2,1)S(1)}, bf16[16,4096]{1,0:T(8,128)(2,1)S(1)}, u32[]{:S(2)}, u32[]{:S(2)}) collective-permute-start(bf16[16,4096]{1,0:T(8,128)(2,1)S(1)} %collective-permute-done.7), channel_id=1, source_target_pairs={{0,1},{1,2},{2,3},{3,4},{4,5},{5,6},{6,7},{7,8},{8,9},{9,10},{10,1... | collective-permute-start | bytes 393224 | tf_op jit(solution)/shard_map/ppermute | solution.py:24
  41.7 9.0 %collective-permute-start.9 = (bf16[16,4096]{1,0:T(8,128)(2,1)S(1)}, bf16[16,4096]{1,0:T(8,128)(2,1)S(1)}, u32[]{:S(2)}, u32[]{:S(2)}) collective-permute-start(bf16[16,4096]{1,0:T(8,128)(2,1)S(1)} %collective-permute-done.8), channel_id=1, source_target_pairs={{0,1},{1,2},{2,3},{3,4},{4,5},{5,6},{6,7},{7,8},{8,9},{9,10},{10,1... | collective-permute-start | bytes 393224 | tf_op jit(solution)/shard_map/ppermute | solution.py:24
  43.9 9.0 %collective-permute-start.16 = (bf16[16,4096]{1,0:T(8,128)(2,1)S(1)}, bf16[16,4096]{1,0:T(8,128)(2,1)S(1)}, u32[]{:S(2)}, u32[]{:S(2)}) collective-permute-start(bf16[16,4096]{1,0:T(8,128)(2,1)S(1)} %collective-permute-done.15), channel_id=1, source_target_pairs={{1,0},{2,1},{3,2},{4,3},{5,4},{6,5},{7,6},{8,7},{9,8},{10,9},{11,1... | collective-permute-start | bytes 393224 | tf_op jit(solution)/shard_map/ppermute | solution.py:26
  50.8 9.0 %collective-permute-start.10 = (bf16[16,4096]{1,0:T(8,128)(2,1)S(1)}, bf16[16,4096]{1,0:T(8,128)(2,1)S(1)}, u32[]{:S(2)}, u32[]{:S(2)}) collective-permute-start(bf16[16,4096]{1,0:T(8,128)(2,1)S(1)} %collective-permute-done.9), channel_id=1, source_target_pairs={{0,1},{1,2},{2,3},{3,4},{4,5},{5,6},{6,7},{7,8},{8,9},{9,10},{10,1... | collective-permute-start | bytes 393224 | tf_op jit(solution)/shard_map/ppermute | solution.py:24
  52.9 9.5 %collective-permute-start.17 = (bf16[16,4096]{1,0:T(8,128)(2,1)S(1)}, bf16[16,4096]{1,0:T(8,128)(2,1)S(1)}, u32[]{:S(2)}, u32[]{:S(2)}) collective-permute-start(bf16[16,4096]{1,0:T(8,128)(2,1)S(1)} %collective-permute-done.16), channel_id=1, source_target_pairs={{1,0},{2,1},{3,2},{4,3},{5,4},{6,5},{7,6},{8,7},{9,8},{10,9},{11,1... | collective-permute-start | bytes 393224 | tf_op jit(solution)/shard_map/ppermute | solution.py:26
  59.8 9.6 %collective-permute-start.11 = (bf16[16,4096]{1,0:T(8,128)(2,1)S(1)}, bf16[16,4096]{1,0:T(8,128)(2,1)S(1)}, u32[]{:S(2)}, u32[]{:S(2)}) collective-permute-start(bf16[16,4096]{1,0:T(8,128)(2,1)S(1)} %collective-permute-done.10), channel_id=1, source_target_pairs={{0,1},{1,2},{2,3},{3,4},{4,5},{5,6},{6,7},{7,8},{8,9},{9,10},{10,1... | collective-permute-start | bytes 393224 | tf_op jit(solution)/shard_map/ppermute | solution.py:24
  62.4 11.5 %collective-permute-start.18 = (bf16[16,4096]{1,0:T(8,128)(2,1)S(1)}, bf16[16,4096]{1,0:T(8,128)(2,1)S(1)}, u32[]{:S(2)}, u32[]{:S(2)}) collective-permute-start(bf16[16,4096]{1,0:T(8,128)(2,1)S(1)} %collective-permute-done.17), channel_id=1, source_target_pairs={{1,0},{2,1},{3,2},{4,3},{5,4},{6,5},{7,6},{8,7},{9,8},{10,9},{11,1... | collective-permute-start | bytes 393224 | tf_op jit(solution)/shard_map/ppermute | solution.py:26
  69.4 14.0 %collective-permute-start.12 = (bf16[16,4096]{1,0:T(8,128)(2,1)S(1)}, bf16[16,4096]{1,0:T(8,128)(2,1)S(1)}, u32[]{:S(2)}, u32[]{:S(2)}) collective-permute-start(bf16[16,4096]{1,0:T(8,128)(2,1)S(1)} %collective-permute-done.11), channel_id=1, source_target_pairs={{0,1},{1,2},{2,3},{3,4},{4,5},{5,6},{6,7},{7,8},{8,9},{9,10},{10,1... | collective-permute-start | bytes 393224 | tf_op jit(solution)/shard_map/ppermute | solution.py:24
  71.3 14.0 %collective-permute-start.4 = (bf16[4,1,32,256]{3,2,1,0:T(8,128)(2,1)S(1)}, bf16[4,1,32,256]{3,2,1,0:T(8,128)(2,1)S(1)}, u32[]{:S(2)}, u32[]{:S(2)}) collective-permute-start(bf16[4,1,32,256]{3,2,1,0:T(8,128)(2,1)S(1)} %get-tuple-element.13), channel_id=1, source_target_pairs={{0,4},{4,8},{8,12},{1,5},{5,9},{9,13},{2,6},{6,10},{10,14},{3,7},{... | collective-permute-start | bytes 196616 | tf_op jit(solution)/shard_map/ppermute | solution.py:40
  72.6 12.7 %collective-permute-start.5 = (bf16[4,1,32,256]{3,2,1,0:T(8,128)(2,1)S(1)}, bf16[4,1,32,256]{3,2,1,0:T(8,128)(2,1)S(1)}, u32[]{:S(2)}, u32[]{:S(2)}) collective-permute-start(bf16[4,1,32,256]{3,2,1,0:T(8,128)(2,1)S(1)} %get-tuple-element.14), channel_id=1, source_target_pairs={{4,0},{8,4},{12,8},{5,1},{9,5},{13,9},{6,2},{10,6},{14,10},{7,3},{... | collective-permute-start | bytes 196616 | tf_op jit(solution)/shard_map/ppermute | solution.py:41
  73.9 16.8 %collective-permute-start.19 = (bf16[16,4096]{1,0:T(8,128)(2,1)S(1)}, bf16[16,4096]{1,0:T(8,128)(2,1)S(1)}, u32[]{:S(2)}, u32[]{:S(2)}) collective-permute-start(bf16[16,4096]{1,0:T(8,128)(2,1)S(1)} %collective-permute-done.18), channel_id=1, source_target_pairs={{1,0},{2,1},{3,2},{4,3},{5,4},{6,5},{7,6},{8,7},{9,8},{10,9},{11,1... | collective-permute-start | bytes 393224 | tf_op jit(solution)/shard_map/ppermute | solution.py:26
  83.3 11.4 %collective-permute-start.13 = (bf16[16,4096]{1,0:T(8,128)(2,1)S(1)}, bf16[16,4096]{1,0:T(8,128)(2,1)S(1)}, u32[]{:S(2)}, u32[]{:S(2)}) collective-permute-start(bf16[16,4096]{1,0:T(8,128)(2,1)S(1)} %collective-permute-done.12), channel_id=1, source_target_pairs={{0,1},{1,2},{2,3},{3,4},{4,5},{5,6},{6,7},{7,8},{8,9},{9,10},{10,1... | collective-permute-start | bytes 393224 | tf_op jit(solution)/shard_map/ppermute | solution.py:24
  85.4 11.3 %collective-permute-start.22 = (bf16[4,18,1,256]{3,2,1,0:T(2,128)(2,1)S(1)}, bf16[4,18,1,256]{3,2,1,0:T(2,128)(2,1)S(1)}, u32[]{:S(2)}, u32[]{:S(2)}) collective-permute-start(bf16[4,18,1,256]{3,2,1,0:T(2,128)(2,1)S(1)} %get-tuple-element.11), channel_id=1, source_target_pairs={{1,0},{2,1},{3,2},{5,4},{6,5},{7,6},{9,8},{10,9},{11,10},{13,12},{... | collective-permute-start | bytes 110600 | tf_op jit(solution)/shard_map/ppermute | solution.py:41
  86.7 10.0 %collective-permute-start.6 = (bf16[4,18,1,256]{3,2,1,0:T(2,128)(2,1)S(1)}, bf16[4,18,1,256]{3,2,1,0:T(2,128)(2,1)S(1)}, u32[]{:S(2)}, u32[]{:S(2)}) collective-permute-start(bf16[4,18,1,256]{3,2,1,0:T(2,128)(2,1)S(1)} %get-tuple-element.12), channel_id=1, source_target_pairs={{0,1},{1,2},{2,3},{4,5},{5,6},{6,7},{8,9},{9,10},{10,11},{12,13},{... | collective-permute-start | bytes 110600 | tf_op jit(solution)/shard_map/ppermute | solution.py:40
  90.7 7.8 %collective-permute-start.20 = (bf16[16,4096]{1,0:T(8,128)(2,1)S(1)}, bf16[16,4096]{1,0:T(8,128)(2,1)S(1)}, u32[]{:S(2)}, u32[]{:S(2)}) collective-permute-start(bf16[16,4096]{1,0:T(8,128)(2,1)S(1)} %collective-permute-done.19), channel_id=1, source_target_pairs={{1,0},{2,1},{3,2},{4,3},{5,4},{6,5},{7,6},{8,7},{9,8},{10,9},{11,1... | collective-permute-start | bytes 393224 | tf_op jit(solution)/shard_map/ppermute | solution.py:26
  94.7 10.4 %collective-permute-start.14 = (bf16[16,4096]{1,0:T(8,128)(2,1)S(1)}, bf16[16,4096]{1,0:T(8,128)(2,1)S(1)}, u32[]{:S(2)}, u32[]{:S(2)}) collective-permute-start(bf16[16,4096]{1,0:T(8,128)(2,1)S(1)} %collective-permute-done.13), channel_id=1, source_target_pairs={{0,1},{1,2},{2,3},{3,4},{4,5},{5,6},{6,7},{7,8},{8,9},{9,10},{10,1... | collective-permute-start | bytes 393224 | tf_op jit(solution)/shard_map/ppermute | solution.py:24
  98.5 16.6 %collective-permute-start.21 = (bf16[16,4096]{1,0:T(8,128)(2,1)S(1)}, bf16[16,4096]{1,0:T(8,128)(2,1)S(1)}, u32[]{:S(2)}, u32[]{:S(2)}) collective-permute-start(bf16[16,4096]{1,0:T(8,128)(2,1)S(1)} %collective-permute-done.20), channel_id=1, source_target_pairs={{1,0},{2,1},{3,2},{4,3},{5,4},{6,5},{7,6},{8,7},{9,8},{10,9},{11,1... | collective-permute-start | bytes 393224 | tf_op jit(solution)/shard_map/ppermute | solution.py:26
  132.6 18.1 %collective-permute-start.23 = (bf16[2,16,32,256]{3,2,1,0:T(8,128)(2,1)S(1)}, bf16[2,16,32,256]{3,2,1,0:T(8,128)(2,1)S(1)}, u32[]{:S(2)}, u32[]{:S(2)}) collective-permute-start(bf16[2,16,32,256]{3,2,1,0:T(8,128)(2,1)S(1)} %slice.199), channel_id=1, source_target_pairs={{0,16},{16,32},{32,48},{48,64},{64,80},{80,96},{96,112},{112,128},... | collective-permute-start | bytes 1572872 | tf_op jit(solution)/shard_map/ppermute | solution.py:49
  160.1 113.5 %all-to-all-start = ((bf16[32,4,16,256]{3,2,1,0:T(8,128)(2,1)}), bf16[32,4,16,256]{3,2,1,0:T(8,128)(2,1)S(1)}, u32[]{:S(2)}, u32[]{:S(2)}) async-start(bf16[32,4,16,256]{3,2,1,0:T(8,128)(2,1)} %bitcast.170), calls=%async_computation | async-start | bytes 2097152 | tf_op jit(solution)/shard_map/all_to_all | solution.py:143
  177.5 94.7 %all-gather.2.cloned.1.call-start = ((), (), s32[]{:S(2)}) async-start(), calls=%async_computation.1 | async-start | bytes 1081344 | tf_op jit(solution)/shard_map/all_gather | solution.py:148
  (12 other events, 154.4 us)
Sparse Core Ops, SparseCore 0:
  200.4 71.7 all-gather.1
